TPU v7x, 256 devices: a whole 4x4x8 slice. The times are simulated.
256 devices in a mesh: embed: 8 (over x, core), hidden: 32 (over y, z).
Axes of the slice: x: 4, y: 4, z: 8, core: 2. Of those that a mesh axis runs over, the one named last changes fastest.
Arguments:
- rows_in: bfloat16 [512, 16384], P('hidden', 'embed'), may hold values from -6 to 6
- gate_weight: bfloat16 [16384, 28672], P('embed', 'hidden'), may hold values from -0.046875 to 0.046875
- up_weight: bfloat16 [16384, 28672], P('embed', 'hidden'), may hold values from -0.046875 to 0.046875
- down_weight: bfloat16 [28672, 16384], P('hidden', 'embed'), may hold values from -0.03125 to 0.03125
Outputs:
- rows_out: bfloat16 [512, 16384], P('hidden', 'embed')
All inputs are finite; a program needn't handle non-finite values.
Results may differ from a plain program's by a relative error of at most 0.0049.
Values may be sent and summed in bfloat16 or wider, within the bound.
No kernel may reach another device: no remote copies, remote signals or barrier semaphores. Data moves between devices by JAX's collectives and lax.ppermute only.
A program may use at most 64 MiB of HBM per device.

v0:
```python
import jax
import jax.numpy as jnp
from jax import lax
from jax.sharding import PartitionSpec as P


def on_device(rows_in, gate_weight, up_weight, down_weight):
    width = gate_weight.shape[1]
    piece = lax.all_gather(rows_in, "hidden", axis=0, tiled=True)
    gate_part = jnp.dot(piece, gate_weight, preferred_element_type=jnp.float32)
    up_part = jnp.dot(piece, up_weight, preferred_element_type=jnp.float32)
    partial_value = jnp.concatenate([gate_part, up_part], axis=1)
    summed = lax.psum(partial_value, "embed")
    activated = (jax.nn.silu(summed[:, :width]) * summed[:, width:]).astype(jnp.bfloat16)
    totals = lax.psum_scatter(
        jnp.dot(activated, down_weight, preferred_element_type=jnp.float32),
        "hidden",
        scatter_dimension=0,
        tiled=True,
    )
    return totals.astype(jnp.bfloat16)


def solution(mesh):
    placed = (
        P("hidden", "embed"),
        P("embed", "hidden"),
        P("embed", "hidden"),
        P("hidden", "embed"),
    )
    return jax.shard_map(
        on_device, mesh=mesh, in_specs=placed, out_specs=P("hidden", "embed"), check_vma=False
    )
```

profile of v0, /device:TPU:2, one launch (start us, length us, event | category | flops | bytes accessed | tf_op | source)
XLA Modules:
  0.0 410.9 jit_solution(4857531397653067271)
XLA Ops:
  6.5 0.0 all-gather.2.cloned.1.call-start
  6.5 0.7 all-gather.2.cloned.1.call-update
  7.3 0.0 all-reduce.2.cloned.1.call-start
  7.3 83.6 %all-gather.2.cloned.1.call-done = bf16[512,2048]{1,0:T(8,128)(2,1)} async-done(((bf16[16,2048]{1,0:T(8,128)(2,1)}), bf16[512,2048]{1,0:T(8,128)(2,1)}) %all-gather.2.cloned.1.call-update) | async-done | bytes 2097168 | tf_op jit(solution)/shard_map/all_gather | solution.py:9
  90.9 0.0 copy-start
  90.9 0.0 copy-start.1
  90.9 5.1 %fusion.6 = f32[512,896]{1,0:T(8,128)S(1)} fusion(bf16[512,2048]{1,0:T(8,128)(2,1)} %all-gather.2.cloned.1.call-done, bf16[2048,896]{1,0:T(8,128)(2,1)} %param.6), kind=kOutput, calls=%fused_computation.7 | convolution fusion | flops 1879048192 | bytes 7602176 | tf_op jit(solution)/shard_map/dot_general | solution.py:11
  96.0 0.0 copy-done
  96.0 0.0 copy-done.1
  96.0 2.3 fusion.5
  98.4 2.1 pad_maximum_fusion
  100.4 0.0 all-reduce.2.cloned.1.call-update
  100.4 0.0 reduce-scatter.2.cloned.1.call-start
  100.5 70.7 %all-reduce.2.cloned.1.call-done = f32[512,1792]{1,0:T(8,128)} async-done(((f32[512,1792]{1,0:T(8,128)}), f32[512,1792]{1,0:T(8,128)}) %all-reduce.2.cloned.1.call-update) | async-done | bytes 3670032 | tf_op jit(solution)/shard_map/psum | solution.py:13
  171.2 7.4 %fusion.1 = f32[512,2048]{1,0:T(8,128)} fusion(bf16[896,2048]{1,0:T(8,128)(2,1)} %param.7, f32[512,1792]{1,0:T(8,128)} %all-reduce.2.cloned.1.call-done), kind=kOutput, calls=%fused_computation.3 | convolution fusion | flops 1881800704 | bytes 11534336 | tf_op jit(solution)/shard_map/dot_general | solution.py:16
  178.6 0.0 reduce-scatter.2.cloned.1.call-update
  178.7 224.2 %reduce-scatter.2.cloned.1.call-done = f32[16,2048]{1,0:T(8,128)} async-done(((f32[512,2048]{1,0:T(8,128)}), f32[16,2048]{1,0:T(8,128)}) %reduce-scatter.2.cloned.1.call-update) | async-done | bytes 131088 | tf_op jit(solution)/shard_map/reduce_scatter | solution.py:15
  402.9 1.5 convert_element_type.7
Async XLA Ops:
  6.5 84.3 %all-gather.2.cloned.1.call-start = ((), (), s32[]{:S(2)}) async-start(), calls=%async_computation.1 | async-start | bytes 2162688 | tf_op jit(solution)/shard_map/all_gather | solution.py:9
  7.3 163.9 %all-reduce.2.cloned.1.call-start = ((), (), s32[]{:S(2)}) async-start(), calls=%async_computation.2 | async-start | bytes 7340032 | tf_op jit(solution)/shard_map/psum | solution.py:13
  90.9 5.2 %copy-start = (bf16[2048,896]{1,0:T(8,128)(2,1)S(1)}, bf16[2048,896]{1,0:T(8,128)(2,1)}, u32[]{:S(2)}) copy-start(bf16[2048,896]{1,0:T(8,128)(2,1)} %param.5) | copy-start | bytes 11010052
  90.9 5.2 %copy-start.1 = (bf16[512,2048]{1,0:T(8,128)(2,1)S(1)}, bf16[512,2048]{1,0:T(8,128)(2,1)}, u32[]{:S(2)}) copy-start(bf16[512,2048]{1,0:T(8,128)(2,1)} %all-gather.2.cloned.1.call-done) | copy-start | bytes 6291460
  100.4 302.4 %reduce-scatter.2.cloned.1.call-start = ((), (), s32[]{:S(2)}) async-start(), calls=%async_computation.3 | async-start | bytes 4325376 | tf_op jit(solution)/shard_map/reduce_scatter | solution.py:15
Sparse Core Ops, SparseCore 0:
  9.9 80.8 all-gather.1
  100.6 70.5 all-reduce.1
  178.8 224.0 reduce-scatter.1
where the time goes:
time: 411 us
  waiting for transfers between devices  379 us (92%)
  matrix products  14.9 us (4%)
  between operations  13.1 us (3%)
    reduce_scatter x1, waiting for transfers between devices, on_device(): lax.psum_scatter(jnp.dot(activated, down_weight, preferred_element_type=j...  224 us
    all_gather x1, waiting for transfers between devices, on_device(): piece = lax.all_gather(rows_in, 'hidden', axis=0, tiled=True)  83.6 us
    psum x1, waiting for transfers between devices, on_device(): summed = lax.psum(partial_value, 'embed')  70.7 us
  transfers between devices with their start and end apart: 3, of which 3 were waited for; matrix products, arithmetic and copies ran while one was open for 0% of the time, Pallas kernels for 0%

commit v1 on v0

--- a/solution.py
+++ b/solution.py
@@ -10,7 +10,7 @@
     gate_part = jnp.dot(piece, gate_weight, preferred_element_type=jnp.float32)
     up_part = jnp.dot(piece, up_weight, preferred_element_type=jnp.float32)
     partial_value = jnp.concatenate([gate_part, up_part], axis=1)
-    summed = lax.psum(partial_value, "embed")
+    summed = jnp.sum(lax.all_gather(partial_value, "embed"), axis=0)
     activated = (jax.nn.silu(summed[:, :width]) * summed[:, width:]).astype(jnp.bfloat16)
     totals = lax.psum_scatter(
         jnp.dot(activated, down_weight, preferred_element_type=jnp.float32),

time: 411 us -> 489 us (1.19)
  waiting for transfers between devices: 379 us -> 445 us
  other arithmetic: 3.6 us -> 16.4 us
    all_gather x0 -> x1, waiting for transfers between devices: none -> 138 us  [on_device(): summed = jnp.sum(lax.all_gather(partial_value, 'embed'), axis=0)]
    psum x1 -> x0, waiting for transfers between devices: 70.7 us -> none  [on_device(): summed = lax.psum(partial_value, 'embed')]
    reduce_sum x0 -> x1, other arithmetic: none -> 12.8 us  [on_device(): summed = jnp.sum(lax.all_gather(partial_value, 'embed'), axis=0)]
where the time goes in v1:
time: 489 us
  waiting for transfers between devices  445 us (91%)
  other arithmetic  16.4 us (3%)
  matrix products  14.9 us (3%)
  between operations  13.1 us (3%)
    reduce_scatter x1, waiting for transfers between devices, on_device(): lax.psum_scatter(jnp.dot(activated, down_weight, preferred_element_type=j...  223 us
    all_gather x1, waiting for transfers between devices, on_device(): summed = jnp.sum(lax.all_gather(partial_value, 'embed'), axis=0)  138 us
    all_gather x1, waiting for transfers between devices, on_device(): piece = lax.all_gather(rows_in, 'hidden', axis=0, tiled=True)  83.6 us
    reduce_sum x1, other arithmetic, on_device(): summed = jnp.sum(lax.all_gather(partial_value, 'embed'), axis=0)  12.8 us
  transfers between devices with their start and end apart: 3, of which 3 were waited for; matrix products, arithmetic and copies ran while one was open for 0% of the time, Pallas kernels for 0%

profile of v1, /device:TPU:2, one launch (start us, length us, event | category | flops | bytes accessed | tf_op | source)
XLA Modules:
  0.0 489.4 jit_solution(11444634483034582942)
XLA Ops:
  6.5 0.0 all-gather.4.cloned.1.call-start
  6.5 0.7 all-gather.4.cloned.1.call-update
  7.3 0.0 all-gather.6.cloned.1.call-start
  7.3 83.6 %all-gather.4.cloned.1.call-done = bf16[512,2048]{1,0:T(8,128)(2,1)} async-done(((bf16[16,2048]{1,0:T(8,128)(2,1)}), bf16[512,2048]{1,0:T(8,128)(2,1)}) %all-gather.4.cloned.1.call-update) | async-done | bytes 2097168 | tf_op jit(solution)/shard_map/all_gather | solution.py:9
  90.9 0.0 copy-start
  90.9 0.0 copy-start.1
  90.9 5.1 %fusion.6 = f32[512,896]{1,0:T(8,128)S(1)} fusion(bf16[512,2048]{1,0:T(8,128)(2,1)} %all-gather.4.cloned.1.call-done, bf16[2048,896]{1,0:T(8,128)(2,1)} %param.6), kind=kOutput, calls=%fused_computation.7 | convolution fusion | flops 1879048192 | bytes 7602176 | tf_op jit(solution)/shard_map/dot_general | solution.py:11
  96.0 0.0 copy-done
  96.0 0.0 copy-done.1
  96.0 2.3 fusion.5
  98.4 2.1 pad_maximum_fusion
  100.4 0.0 all-gather.6.cloned.1.call-update
  100.4 0.0 reduce-scatter.2.cloned.1.call-start
  100.5 138.0 %all-gather.6.cloned.1.call-done = f32[4096,1792]{1,0:T(8,128)} async-done(((f32[512,1792]{1,0:T(8,128)}), f32[4096,1792]{1,0:T(8,128)}) %all-gather.6.cloned.1.call-update) | async-done | bytes 29360144 | tf_op jit(solution)/shard_map/all_gather | solution.py:13
  238.5 12.8 %reduce_sum.9 = f32[512,1792]{1,0:T(8,128)} reduce(f32[8,512,1792]{2,1,0:T(8,128)} %bitcast.6, f32[]{:T(128)} %constant.1.clone.1), dimensions={0}, to_apply=%region_0.0 | reduce | flops 6422528 | bytes 33030148 | tf_op jit(solution)/shard_map/reduce_sum | solution.py:13
  251.2 7.4 %fusion.1 = f32[512,2048]{1,0:T(8,128)} fusion(bf16[896,2048]{1,0:T(8,128)(2,1)} %param.7, f32[512,1792]{1,0:T(8,128)} %reduce_sum.9), kind=kOutput, calls=%fused_computation.3 | convolution fusion | flops 1881800704 | bytes 11534336 | tf_op jit(solution)/shard_map/dot_general | solution.py:16
  258.7 0.0 reduce-scatter.2.cloned.1.call-update
  258.7 222.6 %reduce-scatter.2.cloned.1.call-done = f32[16,2048]{1,0:T(8,128)} async-done(((f32[512,2048]{1,0:T(8,128)}), f32[16,2048]{1,0:T(8,128)}) %reduce-scatter.2.cloned.1.call-update) | async-done | bytes 131088 | tf_op jit(solution)/shard_map/reduce_scatter | solution.py:15
  481.3 1.5 convert_element_type.7
Async XLA Ops:
  6.5 84.3 %all-gather.4.cloned.1.call-start = ((), (), s32[]{:S(2)}) async-start(), calls=%async_computation.1 | async-start | bytes 2162688 | tf_op jit(solution)/shard_map/all_gather | solution.py:9
  7.3 231.2 %all-gather.6.cloned.1.call-start = ((), (), s32[]{:S(2)}) async-start(), calls=%async_computation.3 | async-start | bytes 33030144 | tf_op jit(solution)/shard_map/all_gather | solution.py:13
  90.9 5.2 %copy-start = (bf16[2048,896]{1,0:T(8,128)(2,1)S(1)}, bf16[2048,896]{1,0:T(8,128)(2,1)}, u32[]{:S(2)}) copy-start(bf16[2048,896]{1,0:T(8,128)(2,1)} %param.5) | copy-start | bytes 11010052
  90.9 5.2 %copy-start.1 = (bf16[512,2048]{1,0:T(8,128)(2,1)S(1)}, bf16[512,2048]{1,0:T(8,128)(2,1)}, u32[]{:S(2)}) copy-start(bf16[512,2048]{1,0:T(8,128)(2,1)} %all-gather.4.cloned.1.call-done) | copy-start | bytes 6291460
  100.4 380.9 %reduce-scatter.2.cloned.1.call-start = ((), (), s32[]{:S(2)}) async-start(), calls=%async_computation.2 | async-start | bytes 4325376 | tf_op jit(solution)/shard_map/reduce_scatter | solution.py:15
Sparse Core Ops, SparseCore 0:
  9.9 80.8 all-gather.3
  100.6 137.8 all-gather.5
  258.8 222.4 reduce-scatter.1
